TPU v7x, 256 devices: a whole 4x4x8 slice. The times are simulated.
256 devices in a mesh: dp: 32 (over x, y, core), mp: 8 (over z).
Axes of the slice: x: 4, y: 4, z: 8, core: 2. Of those that a mesh axis runs over, the one named last changes fastest.
Arguments:
- hidden: bfloat16 [512, 1024], P('dp'), may hold values from -6 to 6
- attn_gain: float32 [1024], replicated, may hold values from 0.25 to 1.75
- w_qkv: bfloat16 [1024, 3, 1024], P(None, None, 'mp'), may hold values from -2 to 2
- w_out: bfloat16 [1024, 1024], P('mp'), may hold values from -0.1875 to 0.1875
- mlp_gain: float32 [1024], replicated, may hold values from 0.25 to 1.75
- w_gate_up: bfloat16 [1024, 2, 4096], P(None, None, 'mp'), may hold values from -0.1875 to 0.1875
- w_down: bfloat16 [4096, 1024], P('mp'), may hold values from -0.09375 to 0.09375
- kv_cache: bfloat16 [2, 4096, 128, 1024], P(None, 'dp', None, 'mp'), may hold values from -9 to 9
- lengths: int32 [512], replicated, may hold values from 1 to 16384, as said below
- page_request: int32 [4096], P('dp'), may hold values from -1 to 511, as said below
- page_index: int32 [4096], P('dp'), may hold values from 0 to 127, as said below
Outputs:
- appended: bfloat16 [2, 512, 1024], P(None, 'dp', 'mp')
- hidden_out: bfloat16 [512, 1024], P('dp')
Inputs may be any that keep to these rules, and one draw needn't show every extreme that they name: `lengths`: 4 requests hold exactly 16384 tokens, the others fewer than 512. `page_request`: each request owns exactly ceil(lengths / 128) pool pages, which may lie on any data devices; -1 marks an empty page. `page_index`: the pages of a request carry the places 0 to ceil(lengths / 128) - 1, each once; empty pages carry 0.
All inputs are finite; a program needn't handle non-finite values.
Results may differ from a plain program's by a relative error of at most 0.0085.
Values may be sent and summed in bfloat16 or wider, within the bound.
No kernel may reach another device: no remote copies, remote signals or barrier semaphores. Data moves between devices by JAX's collectives and lax.ppermute only.
A program may use at most 128 MiB of HBM per device.

v0:
```python
import jax
import jax.numpy as jnp
from jax import lax
from jax.sharding import PartitionSpec as P

HEAD_DIM = 64
EPSILON = 1e-05
NEGATIVE = -1e30


def rms_norm(values, gain):
    widened = values.astype(jnp.float32)
    mean_square = jnp.mean(widened * widened, axis=-1, keepdims=True)
    return (widened * lax.rsqrt(mean_square + EPSILON) * gain).astype(jnp.bfloat16)


def body(
    hidden,
    attn_gain,
    w_qkv,
    w_out,
    mlp_gain,
    w_gate_up,
    w_down,
    kv_cache,
    lengths,
    page_request,
    page_index,
):
    local_rows = hidden.shape[0]
    head_cols = w_qkv.shape[2]
    local_heads = head_cols // HEAD_DIM
    pool_pages = kv_cache.shape[1]
    page_len = kv_cache.shape[2]
    data_devices = lax.axis_size("dp")
    requests = local_rows * data_devices
    score_scale = HEAD_DIM ** (-0.5)
    normed = rms_norm(hidden, attn_gain)
    projected = jnp.dot(
        normed, w_qkv.reshape(w_qkv.shape[0], 3 * head_cols), preferred_element_type=jnp.float32
    )
    projected = lax.optimization_barrier(projected.astype(jnp.bfloat16)).reshape(
        local_rows, 3, head_cols
    )
    appended = jnp.stack([projected[:, 1], projected[:, 2]])
    every_query = lax.all_gather(projected[:, 0], "dp", axis=0, tiled=True)
    own_queries = projected[:, 0].reshape(local_rows, local_heads, HEAD_DIM).astype(jnp.float32)
    own_keys = projected[:, 1].reshape(local_rows, local_heads, HEAD_DIM).astype(jnp.float32)
    own_values = projected[:, 2].reshape(local_rows, local_heads, HEAD_DIM).astype(jnp.float32)
    self_scores = jnp.sum(own_queries * own_keys, axis=-1) * score_scale
    home_row = lax.axis_index("dp") * local_rows
    request_ids = jnp.arange(requests, dtype=jnp.int32)
    offsets = jnp.arange(page_len, dtype=jnp.int32)
    owners = page_request
    clamped = jnp.maximum(owners, 0)
    chosen_queries = every_query[clamped].reshape(pool_pages, local_heads, HEAD_DIM)
    key_rows = kv_cache[0].reshape(pool_pages, page_len, local_heads, HEAD_DIM)
    value_rows = kv_cache[1].reshape(pool_pages, page_len, local_heads, HEAD_DIM)
    scores = (
        jnp.einsum("phd,pthd->pht", chosen_queries, key_rows, preferred_element_type=jnp.float32)
        * score_scale
    )
    position = page_index[:, None] * page_len + offsets[None, :]
    usable = (owners[:, None] >= 0) & (position < lengths[clamped][:, None])
    page_max = jnp.max(jnp.where(usable[:, None, :], scores, NEGATIVE), axis=2)
    raw = jnp.where(usable[:, None, :], jnp.exp(scores - page_max[:, :, None]), 0.0)
    page_total = jnp.sum(raw, axis=2)
    page_sum = jnp.einsum(
        "pht,pthd->phd", raw.astype(jnp.bfloat16), value_rows, preferred_element_type=jnp.float32
    )
    member = owners[:, None] == request_ids[None, :]
    seg_max = jnp.max(jnp.where(member[:, :, None], page_max[:, None, :], NEGATIVE), axis=0)
    self_full = lax.dynamic_update_slice(
        jnp.full((requests, local_heads), NEGATIVE, jnp.float32), self_scores, (home_row, 0)
    )
    local_max = jnp.maximum(seg_max, self_full)
    factors = jnp.where(owners[:, None] >= 0, jnp.exp(page_max - local_max[clamped]), 0.0)
    payload = jnp.concatenate(
        [(page_sum * factors[:, :, None]).reshape(pool_pages, head_cols), page_total * factors],
        axis=1,
    )
    onehot = member.astype(jnp.float32)
    local_sums = jnp.einsum("pr,pc->rc", onehot, payload, precision=lax.Precision.HIGHEST)
    home_max = lax.dynamic_slice_in_dim(local_max, home_row, local_rows, 0)
    self_weight = jnp.exp(self_scores - home_max)
    self_payload = jnp.concatenate(
        [(self_weight[:, :, None] * own_values).reshape(local_rows, head_cols), self_weight], axis=1
    )
    local_sums = local_sums + lax.dynamic_update_slice(
        jnp.zeros_like(local_sums), self_payload, (home_row, 0)
    )
    global_max = lax.pmax(local_max, "dp")
    shrink = jnp.exp(local_max - global_max)
    shrink_cols = jnp.concatenate([jnp.repeat(shrink, HEAD_DIM, axis=1), shrink], axis=1)
    mine = lax.psum_scatter(local_sums * shrink_cols, "dp", scatter_dimension=0, tiled=True)
    own_weighted = mine[:, :head_cols].reshape(local_rows, local_heads, HEAD_DIM)
    own_totals = mine[:, head_cols:]
    context = (
        (own_weighted / own_totals[:, :, None]).reshape(local_rows, head_cols).astype(jnp.bfloat16)
    )
    attended = lax.psum(jnp.dot(context, w_out, preferred_element_type=jnp.float32), "mp")
    residual = lax.optimization_barrier(
        (hidden.astype(jnp.float32) + attended).astype(jnp.bfloat16)
    )
    normed_mlp = rms_norm(residual, mlp_gain)
    hidden_cols = w_gate_up.shape[2]
    gate_up = jnp.dot(
        normed_mlp,
        w_gate_up.reshape(w_gate_up.shape[0], 2 * hidden_cols),
        preferred_element_type=jnp.float32,
    ).reshape(local_rows, 2, hidden_cols)
    activated = (jax.nn.silu(gate_up[:, 0]) * gate_up[:, 1]).astype(jnp.bfloat16)
    lowered = lax.psum(jnp.dot(activated, w_down, preferred_element_type=jnp.float32), "mp")
    hidden_out = (residual.astype(jnp.float32) + lowered).astype(jnp.bfloat16)
    return (appended, hidden_out)


def solution(mesh):
    return jax.shard_map(
        body,
        mesh=mesh,
        in_specs=(
            P("dp", None),
            P(),
            P(None, None, "mp"),
            P("mp", None),
            P(),
            P(None, None, "mp"),
            P("mp", None),
            P(None, "dp", None, "mp"),
            P(),
            P("dp"),
            P("dp"),
        ),
        out_specs=(P(None, "dp", "mp"), P("dp", None)),
        check_vma=False,
    )
```

profile of v0, /device:TPU:2, one launch (start us, length us, event | category | flops | bytes accessed | tf_op | source)
XLA Modules:
  0.0 378.3 jit_solution(6640743451332159533)
XLA Ops:
  7.2 0.0 copy-start
  7.2 0.0 reduce-scatter.4.cloned.1.call-start
  7.2 0.7 broadcast_maximum_fusion
  8.0 0.7 broadcast_compare_fusion
  8.6 0.8 iota_compare_fusion
  9.4 1.4 copy.92
  10.8 0.9 fusion.9
  11.7 1.1 convolution_convert_fusion
  12.9 24.7 %all-gather = bf16[512,1,128]{2,0,1:T(8,128)(2,1)S(1)} all-gather(bf16[16,1,128]{2,0,1:T(8,128)(2,1)S(1)} %copy.95), channel_id=2, replica_groups=mesh['dp'=32,'mp'=8] {'dp'}, dimensions={0}, use_global_device_ids=true | all-gather | bytes 135168 | tf_op jit(solution)/shard_map/all_gather | solution.py:46
  37.6 0.7 gather_fusion.1
  38.3 0.1 copy.96
  38.4 0.1 copy.103
  38.6 6.0 %fusion.35 = (bf16[1,128,128,128]{3,2,1,0:T(8,128)(2,1)}, bf16[1,128,128,128]{3,2,1,0:T(8,128)(2,1)}) fusion(bf16[2,128,128,128]{3,2,1,0:T(8,128)(2,1)} %param.18), kind=kLoop, calls=%fused_computation.69 | loop fusion | bytes 16777216 | tf_op jit(solution)/shard_map/slice | solution.py:58
  44.6 6.4 %copy.111 = bf16[1,128,128,128]{2,3,1,0:T(8,128)(2,1)} copy(bf16[1,128,128,128]{3,2,1,0:T(8,128)(2,1)} %get-tuple-element.9) | data formatting | bytes 8388608
  51.0 0.0 copy-done.1
  51.0 1.3 gather_fusion
  52.3 0.0 copy-done.6
  52.3 3.4 fusion.37
  55.7 0.1 fusion.18
  55.8 0.1 select_reduce_fusion.1
  55.9 0.2 fusion.8
  56.1 0.1 select_reduce_fusion
  56.3 0.1 mul.112
  56.3 0.1 reduce_sum.37
  56.4 0.1 copy.99
  56.5 0.1 dynamic_update_slice.6
  56.7 0.1 copy.100
  56.8 0.1 subtract_exponential_fusion.1
  56.9 55.7 %pmax.7 = f32[512,2]{0,1:T(2,128)S(1)} all-reduce(f32[512,2]{0,1:T(2,128)S(1)} %max.9), channel_id=1, replica_groups=mesh['dp'=32,'mp'=8] {'dp'}, use_global_device_ids=true, to_apply=%region_5.6 | all-reduce | flops 1024 | bytes 8192 | tf_op jit(solution)/shard_map/pmax | solution.py:92
  112.6 0.6 gather_fusion.2
  113.2 0.1 copy.101
  113.3 6.4 %copy.112 = bf16[1,128,128,128]{2,3,1,0:T(8,128)(2,1)} copy(bf16[1,128,128,128]{3,2,1,0:T(8,128)(2,1)} %get-tuple-element.8) | data formatting | bytes 8388608
  119.7 4.6 %fusion = f32[128,2,1,64]{3,2,1,0:T(1,128)S(1)} fusion(bf16[128,128,2,64]{1,3,2,0:T(8,128)(2,1)} %bitcast.70, bf16[128,2,128,1]{2,0,1,3:T(8,128)(2,1)S(1)} %get-tuple-element.10), kind=kOutput, calls=%fused_computation.8 | convolution fusion | flops 4194304 | bytes 4325376 | tf_op jit(solution)/shard_map/pht,pthd->phd/dot_general | solution.py:68
  124.3 0.1 copy.106
  124.4 0.1 copy.110
  124.5 0.4 fusion.4
  124.9 0.1 maximum_add_fusion
  125.0 0.7 add.66
  125.8 0.8 maximum_multiply_fusion
  126.5 1.9 copy.107
  128.5 0.0 reduce-scatter.4.cloned.1.call-update
  128.5 0.0 all-reduce.3.cloned.1.call-start
  128.6 92.6 %reduce-scatter.4.cloned.1.call-done = f32[16,130]{1,0:T(8,128)} async-done(((f32[512,130]{1,0:T(8,128)}), f32[16,130]{1,0:T(8,128)}) %reduce-scatter.4.cloned.1.call-update) | async-done | bytes 8336
  221.2 0.7 slice.48
  221.9 0.1 copy.113
  222.0 0.7 slice.49
  222.7 0.1 copy.114
  222.8 1.8 fusion.38
  224.5 0.0 all-reduce.3.cloned.1.call-update
  224.6 0.0 all-reduce.5.cloned.1.call-start
  224.6 0.0 copy-done.2
  224.6 0.0 copy-start.3
  224.6 0.0 copy-start.4
  224.7 1.9 copy.116
  226.6 2.9 copy.102
  229.5 67.3 %all-reduce.3.cloned.1.call-done = f32[16,1024]{1,0:T(8,128)} async-done(((f32[16,1024]{1,0:T(8,128)}), f32[16,1024]{1,0:T(8,128)}) %all-reduce.3.cloned.1.call-update) | async-done | bytes 65552 | tf_op jit(solution)/shard_map/psum | solution.py:101
  296.8 0.8 fusion.12
  297.6 0.1 fusion.13
  297.8 0.6 fusion.20
  298.4 0.9 fusion.29
  299.3 0.0 all-reduce.5.cloned.1.call-update
  299.3 0.6 pad_maximum_fusion
  299.9 70.4 %all-reduce.5.cloned.1.call-done = f32[16,1024]{1,0:T(8,128)} async-done(((f32[16,1024]{1,0:T(8,128)}), f32[16,1024]{1,0:T(8,128)}) %all-reduce.5.cloned.1.call-update) | async-done | bytes 65552 | tf_op jit(solution)/shard_map/psum | solution.py:113
  370.3 1.5 fusion.16
  (26 shorter events, 0.2 us)
Async XLA Ops:
  7.2 291.2 %copy-start = (bf16[512,1024]{1,0:T(8,128)(2,1)S(1)}, bf16[512,1024]{1,0:T(8,128)(2,1)}, u32[]{:S(2)}) copy-start(bf16[512,1024]{1,0:T(8,128)(2,1)} %param.17) | copy-start | bytes 3145732
  7.2 214.0 %reduce-scatter.4.cloned.1.call-start = ((), (), s32[]{:S(2)}) async-start(), calls=%async_computation.3 | async-start | bytes 540672
  44.6 6.4 %copy-start.1 = (s32[512]{0:T(512)S(1)}, s32[512]{0:T(512)}, u32[]{:S(2)}) copy-start(s32[512]{0:T(512)} %param.19) | copy-start | bytes 6148
  44.6 7.7 %copy-start.6 = (s32[128]{0:T(128)S(1)}, s32[128]{0:T(128)}, u32[]{:S(2)}) copy-start(s32[128]{0:T(128)} %param.21) | copy-start | bytes 1540
  119.7 4.9 %copy-start.5 = (s32[128]{0:T(128)S(1)}, s32[128]{0:T(128)}, u32[]{:S(2)}) copy-start(s32[128]{0:T(128)} %param.20) | copy-start | bytes 1540
  119.7 104.9 %copy-start.2 = (bf16[1024,2,512]{2,1,0:T(2,128)(2,1)S(1)}, bf16[1024,2,512]{2,1,0:T(2,128)(2,1)}, u32[]{:S(2)}) copy-start(bf16[1024,2,512]{2,1,0:T(2,128)(2,1)} %param.16) | copy-start | bytes 6291460
  128.5 168.3 %all-reduce.3.cloned.1.call-start = ((), (), s32[]{:S(2)}) async-start(), calls=%async_computation.1 | async-start | bytes 131072 | tf_op jit(solution)/shard_map/psum | solution.py:101
  224.6 145.8 %all-reduce.5.cloned.1.call-start = ((), (), s32[]{:S(2)}) async-start(), calls=%async_computation.2 | async-start | bytes 131072 | tf_op jit(solution)/shard_map/psum | solution.py:113
  224.6 72.1 %copy-start.3 = (bf16[16,1024]{1,0:T(8,128)(2,1)S(1)}, bf16[16,1024]{1,0:T(8,128)(2,1)}, u32[]{:S(2)}) copy-start(bf16[16,1024]{1,0:T(8,128)(2,1)} %param.11) | copy-start | bytes 98308
  224.6 73.1 %copy-start.4 = (f32[1024]{0:T(1024)S(1)}, f32[1024]{0:T(1024)}, u32[]{:S(2)}) copy-start(f32[1024]{0:T(1024)} %param.15) | copy-start | bytes 12292
Sparse Core Ops, SparseCore 0:
  128.6 92.5 reduce-scatter.3
  224.7 72.0 all-reduce.2
  299.4 70.8 all-reduce.4
where the time goes:
time: 379 us; the launch traced here: 378 us
  waiting for transfers between devices  230 us (61%)
  blocking collectives  80.4 us (21%)
  local copies, waits for them, and re-layouts  32.9 us (9%)
  between operations  14 us (4%)
  matrix products  12.7 us (3%)
  other arithmetic  7.77 us (2%)
    unnamed x4, waiting for transfers between devices  92.7 us
    psum x1, waiting for transfers between devices, body(): lax.psum(jnp.dot(activated, w_down, preferred_element_type=jnp.float32),...  70.4 us
    psum x1, waiting for transfers between devices, body(): lax.psum(jnp.dot(context, w_out, preferred_element_type=jnp.float32), 'mp')  67.3 us
    pmax x1, blocking collectives, body(): global_max = lax.pmax(local_max, 'dp')  55.7 us
    all_gather x1, blocking collectives, body(): every_query = lax.all_gather(projected[:, 0], 'dp', axis=0, tiled=True)  24.7 us
    unnamed x22, local copies, waits for them, and re-layouts  18.4 us
  transfers between devices with their start and end apart: 3, of which 3 were waited for; matrix products, arithmetic and copies ran while one was open for 1% of the time, Pallas kernels for 0%

commit v1 on v0

--- a/solution.py
+++ b/solution.py
@@ -43,7 +43,13 @@
         local_rows, 3, head_cols
     )
     appended = jnp.stack([projected[:, 1], projected[:, 2]])
-    every_query = lax.all_gather(projected[:, 0], "dp", axis=0, tiled=True)
+    w_in = projected[:, 0]
+    every_query = jnp.concatenate(
+        lax.all_to_all(
+            jnp.stack(lax.axis_size("dp") * [w_in], 0), concat_axis=0, axis_name="dp", split_axis=0
+        ),
+        0,
+    )
     own_queries = projected[:, 0].reshape(local_rows, local_heads, HEAD_DIM).astype(jnp.float32)
     own_keys = projected[:, 1].reshape(local_rows, local_heads, HEAD_DIM).astype(jnp.float32)
     own_values = projected[:, 2].reshape(local_rows, local_heads, HEAD_DIM).astype(jnp.float32)

time: 379 us -> 365 us (0.963)
  blocking collectives: 80.4 us -> 55.5 us
  starting transfers between devices: 0.12 us -> 7.75 us
    all_gather x1 -> x0, blocking collectives: 24.7 us -> none  [body(): every_query = lax.all_gather(projected[:, 0], 'dp', axis=0, tiled=True)]
    all_to_all x0 -> x1, starting transfers between devices: none -> 7.62 us  [body(): lax.all_to_all(jnp.stack(lax.axis_size('dp') * [w_in], 0), concat_axis=0,...]
    unnamed x22 -> x23, local copies, waits for them, and re-layouts: 18.4 us -> 18.5 us
  transfers between devices with their start and end apart: 3 -> 4, of which waited for: 3 -> 3; matrix products, arithmetic and copies ran while one was open for 1% -> 8% of each run, Pallas kernels for 0% -> 0%
where the time goes in v1:
time: 365 us; the launch traced here: 364 us
  waiting for transfers between devices  232 us (64%)
  blocking collectives  55.5 us (15%)
  local copies, waits for them, and re-layouts  33.8 us (9%)
  between operations  14 us (4%)
  matrix products  12.7 us (3%)
  starting transfers between devices  7.75 us (2%)
  other arithmetic  7.7 us (2%)
    unnamed x4, waiting for transfers between devices  94.6 us
    psum x1, waiting for transfers between devices, body(): lax.psum(jnp.dot(activated, w_down, preferred_element_type=jnp.float32),...  70.4 us
    psum x1, waiting for transfers between devices, body(): lax.psum(jnp.dot(context, w_out, preferred_element_type=jnp.float32), 'mp')  67.3 us
    pmax x1, blocking collectives, body(): global_max = lax.pmax(local_max, 'dp')  55.5 us
    unnamed x23, local copies, waits for them, and re-layouts  18.5 us
    all_to_all x1, starting transfers between devices, body(): lax.all_to_all(jnp.stack(lax.axis_size('dp') * [w_in], 0), concat_axis=0,...  7.62 us
  transfers between devices with their start and end apart: 4, of which 3 were waited for; matrix products, arithmetic and copies ran while one was open for 8% of the time, Pallas kernels for 0%

profile of v1, /device:TPU:2, one launch (start us, length us, event | category | flops | bytes accessed | tf_op | source)
XLA Modules:
  0.0 363.8 jit_solution(1156278792572877418)
XLA Ops:
  7.2 0.0 copy-start
  7.2 1.5 copy.88
  8.7 0.9 fusion.9
  9.6 1.1 convolution_convert_fusion
  10.7 0.7 stack.7
  11.4 7.6 %all-to-all-start = ((bf16[32,16,128]{2,1,0:T(8,128)(2,1)}), bf16[32,16,128]{2,1,0:T(8,128)(2,1)S(1)}, u32[]{:S(2)}, u32[]{:S(2)}) async-start(bf16[32,16,128]{2,1,0:T(8,128)(2,1)} %stack.7), calls=%async_computation | async-start | bytes 262144 | tf_op jit(solution)/shard_map/all_to_all | solution.py:48
  19.0 0.0 reduce-scatter.4.cloned.1.call-start
  19.1 0.7 broadcast_maximum_fusion
  19.7 0.7 broadcast_compare_fusion
  20.4 0.8 iota_compare_fusion
  21.2 6.1 %fusion.35 = (bf16[1,128,128,128]{3,2,1,0:T(8,128)(2,1)}, bf16[1,128,128,128]{3,2,1,0:T(8,128)(2,1)}) fusion(bf16[2,128,128,128]{3,2,1,0:T(8,128)(2,1)} %param.18), kind=kLoop, calls=%fused_computation.70 | loop fusion | bytes 16777216 | tf_op jit(solution)/shard_map/slice | solution.py:64
  27.3 6.4 %copy.107 = bf16[1,128,128,128]{2,3,1,0:T(8,128)(2,1)} copy(bf16[1,128,128,128]{3,2,1,0:T(8,128)(2,1)} %get-tuple-element.9) | data formatting | bytes 8388608
  33.7 0.0 copy-done.6
  33.7 0.1 mul.112
  33.8 0.1 reduce_sum.37
  33.9 0.1 copy.94
  34.0 6.4 %copy.108 = bf16[1,128,128,128]{2,3,1,0:T(8,128)(2,1)} copy(bf16[1,128,128,128]{3,2,1,0:T(8,128)(2,1)} %get-tuple-element.8) | data formatting | bytes 8388608
  40.3 0.1 copy.106
  40.5 1.3 gather_fusion
  41.8 0.2 dynamic_update_slice.6
  41.9 0.1 fusion.18
  42.1 0.0 all-to-all-done
  42.1 0.7 gather_fusion.1
  42.8 0.1 copy.91
  42.9 0.1 copy.98
  43.0 3.4 fusion.37
  46.4 0.1 select_reduce_fusion.1
  46.5 0.2 fusion.8
  46.7 0.1 select_reduce_fusion
  46.9 0.1 copy.95
  47.0 0.1 subtract_exponential_fusion.1
  47.1 55.5 %pmax.7 = f32[512,2]{0,1:T(2,128)S(1)} all-reduce(f32[512,2]{0,1:T(2,128)S(1)} %max.9), channel_id=1, replica_groups=mesh['dp'=32,'mp'=8] {'dp'}, use_global_device_ids=true, to_apply=%region_5.6 | all-reduce | flops 1024 | bytes 8192 | tf_op jit(solution)/shard_map/pmax | solution.py:98
  102.6 0.6 gather_fusion.2
  103.2 0.1 copy.96
  103.3 4.6 %fusion = f32[128,2,1,64]{3,2,1,0:T(1,128)S(1)} fusion(bf16[128,128,2,64]{1,3,2,0:T(8,128)(2,1)} %bitcast.73, bf16[128,2,128,1]{2,0,1,3:T(8,128)(2,1)S(1)} %get-tuple-element.10), kind=kOutput, calls=%fused_computation.8 | convolution fusion | flops 4194304 | bytes 4325376 | tf_op jit(solution)/shard_map/pht,pthd->phd/dot_general | solution.py:74
  107.9 0.1 copy.101
  108.0 0.4 fusion.4
  108.4 0.1 maximum_add_fusion
  108.5 0.7 add.66
  109.3 0.8 maximum_multiply_fusion
  110.0 1.9 copy.102
  112.0 0.0 reduce-scatter.4.cloned.1.call-update
  112.0 0.0 all-reduce.3.cloned.1.call-start
  112.0 94.6 %reduce-scatter.4.cloned.1.call-done = f32[16,130]{1,0:T(8,128)} async-done(((f32[512,130]{1,0:T(8,128)}), f32[16,130]{1,0:T(8,128)}) %reduce-scatter.4.cloned.1.call-update) | async-done | bytes 8336
  206.6 0.7 slice.48
  207.3 0.1 copy.109
  207.4 0.7 slice.49
  208.1 0.1 copy.110
  208.2 1.8 fusion.38
  210.0 0.0 all-reduce.3.cloned.1.call-update
  210.0 0.0 all-reduce.5.cloned.1.call-start
  210.1 0.0 copy-start.3
  210.1 0.0 copy-start.4
  210.1 1.9 copy.112
  212.0 2.9 copy.97
  214.9 67.3 %all-reduce.3.cloned.1.call-done = f32[16,1024]{1,0:T(8,128)} async-done(((f32[16,1024]{1,0:T(8,128)}), f32[16,1024]{1,0:T(8,128)}) %all-reduce.3.cloned.1.call-update) | async-done | bytes 65552 | tf_op jit(solution)/shard_map/psum | solution.py:107
  282.2 0.8 fusion.12
  283.1 0.1 fusion.13
  283.2 0.6 fusion.20
  283.9 0.9 fusion.29
  284.8 0.0 all-reduce.5.cloned.1.call-update
  284.8 0.6 pad_maximum_fusion
  285.4 70.4 %all-reduce.5.cloned.1.call-done = f32[16,1024]{1,0:T(8,128)} async-done(((f32[16,1024]{1,0:T(8,128)}), f32[16,1024]{1,0:T(8,128)}) %all-reduce.5.cloned.1.call-update) | async-done | bytes 65552 | tf_op jit(solution)/shard_map/psum | solution.py:119
  355.8 1.5 fusion.16
  (28 shorter events, 0.2 us)
Async XLA Ops:
  7.2 276.7 %copy-start = (bf16[512,1024]{1,0:T(8,128)(2,1)S(1)}, bf16[512,1024]{1,0:T(8,128)(2,1)}, u32[]{:S(2)}) copy-start(bf16[512,1024]{1,0:T(8,128)(2,1)} %param.17) | copy-start | bytes 3145732
  11.4 30.7 %all-to-all-start = ((bf16[32,16,128]{2,1,0:T(8,128)(2,1)}), bf16[32,16,128]{2,1,0:T(8,128)(2,1)S(1)}, u32[]{:S(2)}, u32[]{:S(2)}) async-start(bf16[32,16,128]{2,1,0:T(8,128)(2,1)} %stack.7), calls=%async_computation | async-start | bytes 262144 | tf_op jit(solution)/shard_map/all_to_all | solution.py:48
  19.0 187.6 %reduce-scatter.4.cloned.1.call-start = ((), (), s32[]{:S(2)}) async-start(), calls=%async_computation.4 | async-start | bytes 540672
  27.3 6.4 %copy-start.6 = (s32[128]{0:T(128)S(1)}, s32[128]{0:T(128)}, u32[]{:S(2)}) copy-start(s32[128]{0:T(128)} %param.21) | copy-start | bytes 1540
  34.0 6.5 %copy-start.1 = (s32[512]{0:T(512)S(1)}, s32[512]{0:T(512)}, u32[]{:S(2)}) copy-start(s32[512]{0:T(512)} %param.19) | copy-start | bytes 6148
  46.4 61.6 %copy-start.5 = (s32[128]{0:T(128)S(1)}, s32[128]{0:T(128)}, u32[]{:S(2)}) copy-start(s32[128]{0:T(128)} %param.20) | copy-start | bytes 1540
  103.3 106.8 %copy-start.2 = (bf16[1024,2,512]{2,1,0:T(2,128)(2,1)S(1)}, bf16[1024,2,512]{2,1,0:T(2,128)(2,1)}, u32[]{:S(2)}) copy-start(bf16[1024,2,512]{2,1,0:T(2,128)(2,1)} %param.16) | copy-start | bytes 6291460
  112.0 170.2 %all-reduce.3.cloned.1.call-start = ((), (), s32[]{:S(2)}) async-start(), calls=%async_computation.2 | async-start | bytes 131072 | tf_op jit(solution)/shard_map/psum | solution.py:107
  210.0 145.8 %all-reduce.5.cloned.1.call-start = ((), (), s32[]{:S(2)}) async-start(), calls=%async_computation.3 | async-start | bytes 131072 | tf_op jit(solution)/shard_map/psum | solution.py:119
  210.1 72.1 %copy-start.3 = (bf16[16,1024]{1,0:T(8,128)(2,1)S(1)}, bf16[16,1024]{1,0:T(8,128)(2,1)}, u32[]{:S(2)}) copy-start(bf16[16,1024]{1,0:T(8,128)(2,1)} %param.11) | copy-start | bytes 98308
  210.1 73.1 %copy-start.4 = (f32[1024]{0:T(1024)S(1)}, f32[1024]{0:T(1024)}, u32[]{:S(2)}) copy-start(f32[1024]{0:T(1024)} %param.15) | copy-start | bytes 12292
Sparse Core Ops, SparseCore 0:
  112.1 94.4 reduce-scatter.3
  210.1 72.0 all-reduce.2
  284.9 70.8 all-reduce.4
